TPU v7x, 32 devices: a whole 2x2x4 slice. The times are simulated.
32 devices in a mesh: dp: 8 (over y, x, core), fsdp: 4 (over z).
Axes of the slice: x: 2, y: 2, z: 4, core: 2. Of those that a mesh axis runs over, the one named last changes fastest.
Arguments:
- query_cache: bfloat16 [384, 1024], P('dp', 'fsdp'), may hold values from -8 to 8
- region_cache: bfloat16 [384, 1024], P('dp', 'fsdp'), may hold values from -8 to 8
- positive: int32 [384], P('dp'), may hold values from 0 to 383, each once
- hidden_states: bfloat16 [4096, 4096], P(('dp', 'fsdp')), may hold values from -12 to 12
- segment_ids: int32 [8, 512], P('dp', 'fsdp'), may hold values from 0 to 47, never falling along the last dimension, each value on 1 to 21 neighbouring positions
- norm_gain: bfloat16 [4096], replicated, may hold values from 0.099609375 to 1.8984375
- proj_weight: bfloat16 [4096, 1024], P('fsdp'), may hold values from -1 to 1
Outputs:
- mean_loss: float32 [], replicated
- query_grad: float32 [384, 1024], P('dp', 'fsdp')
- region_grad: float32 [384, 1024], P('dp', 'fsdp')
- hidden_grad: bfloat16 [4096, 4096], P(('dp', 'fsdp'))
- gain_grad: float32 [4096], replicated
- proj_grad: float32 [4096, 1024], P('dp', 'fsdp')
Inputs may be any that keep to these rules, and one draw needn't show every extreme that they name: Each region is the positive of exactly one instruction. `segment_ids`: within a pair group the ids never fall, every instruction has at least one token, and one has exactly 21.
All inputs are finite; a program needn't handle non-finite values.
Results may differ from a plain program's by a relative error of at most 0.0088.
Values may be sent and summed in bfloat16 or wider, within the bound.
No kernel may reach another device: no remote copies, remote signals or barrier semaphores. Data moves between devices by JAX's collectives and lax.ppermute only.
A program may use at most 64 MiB of HBM per device.

v0:
```python
import jax
import jax.numpy as jnp
from jax import lax
from jax.sharding import PartitionSpec as P

E = 1024
EPS = 1e-05


def local(query_cache, region_cache, positive, hidden_states, segment_ids, norm_gain, proj_weight):
    row_count = query_cache.shape[0]
    data_count = lax.axis_size("dp")
    pair_count = row_count * data_count
    logit_scale = float(E) ** (-0.5)
    contract_last = (((1,), (1,)), ((), ()))
    contract_first = (((0,), (0,)), ((), ()))
    region_all, query_all = (
        lax.all_gather(region_cache, "dp", axis=0, tiled=True),
        lax.all_gather(query_cache, "dp", axis=0, tiled=True),
    )
    partial_value = lax.dot_general(
        query_cache, region_all, contract_last, preferred_element_type=jnp.float32
    )
    scores = lax.psum(partial_value, "fsdp") * logit_scale
    row_max = jnp.max(scores, axis=1, keepdims=True)
    log_total = row_max[:, 0] + jnp.log(jnp.sum(jnp.exp(scores - row_max), axis=1))
    columns = lax.broadcasted_iota(jnp.int32, (1, pair_count), 1)
    matched = columns == positive[:, None]
    target_score = jnp.sum(jnp.where(matched, scores, jnp.zeros_like(scores)), axis=1)
    loss_local = jnp.sum(log_total - target_score)
    grad_probs = (jnp.exp(scores - log_total[:, None]) - matched.astype(jnp.float32)).astype(
        jnp.bfloat16
    )
    query_grad = logit_scale * jnp.dot(grad_probs, region_all, preferred_element_type=jnp.float32)
    totals_all, targets_all = (
        lax.all_gather(log_total, "dp", axis=0, tiled=True),
        lax.all_gather(positive.astype(jnp.float32), "dp", axis=0, tiled=True),
    )
    partial_t = lax.dot_general(
        region_cache, query_all, contract_last, preferred_element_type=jnp.float32
    )
    scores_t = lax.psum(partial_t, "fsdp") * logit_scale
    own_rows = (
        lax.axis_index("dp") * row_count + lax.broadcasted_iota(jnp.int32, (row_count, 1), 0)
    ).astype(jnp.float32)
    matched_t = targets_all[None, :] == own_rows
    probs_t = (jnp.exp(scores_t - totals_all[None, :]) - matched_t.astype(jnp.float32)).astype(
        jnp.bfloat16
    )
    region_grad = logit_scale * jnp.dot(probs_t, query_all, preferred_element_type=jnp.float32)
    gain = norm_gain.astype(jnp.float32)
    states = hidden_states.astype(jnp.float32)
    inv_rms = lax.rsqrt(jnp.mean(states * states, axis=1, keepdims=True) + EPS)
    normed = (states * inv_rms * gain).astype(jnp.bfloat16)
    labels = lax.broadcasted_iota(jnp.int32, (row_count, 1), 0)
    member = segment_ids[0][None, :] == labels
    pooled_part = jnp.dot(member.astype(jnp.bfloat16), normed, preferred_element_type=jnp.float32)
    counts_part = jnp.sum(member.astype(jnp.float32), axis=1)
    pooled, counts = lax.psum((pooled_part, counts_part), "fsdp")
    mean_pooled = (pooled / counts[:, None]).astype(jnp.bfloat16)
    grad_low = query_grad.astype(jnp.bfloat16)
    grad_full = lax.all_gather(grad_low, "fsdp", axis=1, tiled=True)
    mean_part = lax.dot_general(
        grad_full, proj_weight, contract_last, preferred_element_type=jnp.float32
    )
    mean_grad = lax.all_gather(mean_part, "fsdp", axis=1, tiled=True)
    pool_grad = mean_grad / counts[:, None]
    normed_grad = lax.dot_general(
        member.astype(jnp.float32),
        pool_grad,
        contract_first,
        precision=lax.Precision.HIGHEST,
        preferred_element_type=jnp.float32,
    )
    gain_part = jnp.sum(normed_grad * states * inv_rms, axis=0)
    scaled = gain * normed_grad
    inner = jnp.mean(scaled * states, axis=1, keepdims=True)
    hidden_grad = (inv_rms * scaled - states * inv_rms**3 * inner).astype(jnp.bfloat16)
    proj_grad = lax.psum_scatter(
        lax.dot_general(mean_pooled, grad_low, contract_first, preferred_element_type=jnp.float32),
        "dp",
        scatter_dimension=0,
        tiled=True,
    )
    loss_total = lax.psum(loss_local, "dp")
    gain_grad = lax.psum(gain_part, ("dp", "fsdp"))
    mean_loss = loss_total / pair_count
    return (mean_loss, query_grad, region_grad, hidden_grad, gain_grad, proj_grad)


def solution(mesh):
    in_specs = (
        P("dp", "fsdp"),
        P("dp", "fsdp"),
        P("dp"),
        P(("dp", "fsdp"), None),
        P("dp", "fsdp"),
        P(),
        P("fsdp", None),
    )
    out_specs = (
        P(),
        P("dp", "fsdp"),
        P("dp", "fsdp"),
        P(("dp", "fsdp"), None),
        P(),
        P("dp", "fsdp"),
    )
    return jax.shard_map(local, mesh=mesh, in_specs=in_specs, out_specs=out_specs, check_vma=False)
```

profile of v0, /device:TPU:12, one launch (start us, length us, event | category | flops | bytes accessed | tf_op | source)
XLA Modules:
  0.0 194.4 jit_solution(16001850921238040908)
XLA Ops:
  7.2 0.0 all-reduce.6.cloned.1.call-start
  7.2 1.7 fusion
  8.9 0.6 multiply_multiply_fusion
  9.5 0.7 convert_element_type.53
  10.2 9.2 %all_gather.19 = bf16[384,256]{1,0:T(8,128)(2,1)S(1)} all-gather(bf16[48,256]{1,0:T(8,128)(2,1)} %param.7), channel_id=1, replica_groups=mesh['dp'=8,'fsdp'=4] {'dp'}, dimensions={0}, use_global_device_ids=true | all-gather | bytes 221184 | tf_op jit(solution)/shard_map/all_gather | solution.py:19
  19.5 8.5 %all_gather.18 = bf16[384,256]{1,0:T(8,128)(2,1)S(1)} all-gather(bf16[48,256]{1,0:T(8,128)(2,1)} %param.8), channel_id=1, replica_groups=mesh['dp'=8,'fsdp'=4] {'dp'}, dimensions={0}, use_global_device_ids=true | all-gather | bytes 221184 | tf_op jit(solution)/shard_map/all_gather | solution.py:18
  27.9 1.6 fusion.32
  29.5 1.6 fusion.31
  31.1 1.4 fusion.9
  32.4 0.0 reduce-scatter.2.cloned.1.call-start
  32.5 1.2 dynamic-slice
  34.4 1.3 convert_reduce_fusion
  35.7 9.7 %psum.45 = f32[48]{0:T(128)} all-reduce(f32[48]{0:T(128)} %convert_reduce_fusion), channel_id=1, replica_groups=mesh['dp'=8,'fsdp'=4] {'fsdp'}, use_global_device_ids=true, to_apply=%region_9.10 | all-reduce | flops 48 | bytes 384 | tf_op jit(solution)/shard_map/psum | solution.py:59
  45.4 37.4 %all-reduce.6.cloned.1.call-done = (f32[48,384]{1,0:T(8,128)}, f32[48,384]{1,0:T(8,128)}, f32[48,4096]{1,0:T(8,128)}) async-done(((f32[48,384]{1,0:T(8,128)}, f32[48,384]{1,0:T(8,128)}, f32[48,4096]{1,0:T(8,128)}), (f32[48,384]{1,0:T(8,128)}, f32[48,384]{1,0:T(8,128)}, f32[48,4096]{1,0:T(8,128)})) %all-reduce.6.cloned.1.call-update) | async-done | bytes 933904 | tf_op jit(solution)/shard_map/psum | solution.py:24
  82.8 1.0 multiply_reduce_fusion
  83.8 1.6 select_reduce_fusion
  85.4 0.1 fusion.29
  85.5 1.7 fusion.30
  87.2 0.6 copy-done.2
  87.9 3.9 %fusion.15 = f32[4096,256]{1,0:T(8,128)} fusion(bf16[48,256]{1,0:T(8,128)(2,1)S(1)} %get-tuple-element.20, f32[48,4096]{1,0:T(8,128)} %get-tuple-element.15, f32[48]{0:T(128)} %psum.45), kind=kOutput, calls=%fused_computation.22 | convolution fusion | flops 101056512 | bytes 5005504 | tf_op jit(solution)/shard_map/dot_general | solution.py:80
  91.8 0.0 reduce-scatter.2.cloned.1.call-update
  91.9 0.5 copy-done.7
  92.4 0.1 convert_dynamic-update-slice_fusion
  92.5 0.6 subtract_reduce_fusion
  93.1 13.3 %all-reduce.2 = (f32[]{:T(128)}, f32[384]{0:T(512)S(1)}, f32[384]{0:T(512)S(1)}) all-reduce(f32[]{:T(128)} %subtract_reduce_fusion, f32[384]{0:T(512)S(1)} %convert_dynamic-update-slice_fusion, f32[384]{0:T(512)S(1)} %copy-done.6), channel_id=1, replica_groups=mesh['dp'=8,'fsdp'=4] {'dp'}, use_global_device_ids=true, to_apply=%region_5.6 | all-reduce | flops 769 | bytes 6152 | tf_op jit(solution)/shard_map/psum | solution.py:85
  107.1 12.2 %all_gather.22 = bf16[48,1024]{1,0:T(8,128)(2,1)S(1)} all-gather(bf16[48,256]{1,0:T(8,128)(2,1)S(1)} %copy-done.3), channel_id=1, replica_groups=mesh['dp'=8,'fsdp'=4] {'fsdp'}, dimensions={1}, use_global_device_ids=true | all-gather | bytes 122880 | tf_op jit(solution)/shard_map/all_gather | solution.py:62
  119.3 0.7 fusion.33
  120.0 17.5 %all_gather.23 = f32[48,4096]{1,0:T(8,128)S(1)} all-gather(f32[48,1024]{1,0:T(8,128)S(1)} %fusion.33), channel_id=1, replica_groups=mesh['dp'=8,'fsdp'=4] {'fsdp'}, dimensions={1}, use_global_device_ids=true | all-gather | bytes 983040 | tf_op jit(solution)/shard_map/all_gather | solution.py:66
  137.6 2.8 %fusion.6 = (f32[4096]{0:T(1024)S(1)}, f32[128]{0:T(128)S(1)}, f32[128,4096]{1,0:T(8,128)}) fusion(bf16[128,4096]{1,0:T(8,128)(2,1)S(1)} %copy-done.1, f32[128]{0:T(128)S(1)} %copy-done.12, f32[4096]{0:T(1024)S(1)} %convert_element_type.53, f32[48,4096]{1,0:T(8,128)S(1)} %all_gather.23, f32[48]{0:T(128)S(1)} %copy-done.13, s32[128]{0:T(128)S(1)} %bitcast.13), kind=kOutput, calls=%fused_computation.11 | convolution fusion | flops 305858432 | bytes 3966656 | tf_op jit(solution)/shard_map/dot_general | solution.py:68
  140.4 42.0 %psum.46 = f32[4096]{0:T(1024)} all-reduce(f32[4096]{0:T(1024)S(1)} %get-tuple-element.6), channel_id=1, replica_groups=mesh['dp'=8,'fsdp'=4] {'dp','fsdp'}, use_global_device_ids=true, to_apply=%region_12.13 | all-reduce | flops 4096 | bytes 32768 | tf_op jit(solution)/shard_map/psum | solution.py:86
  182.5 0.8 convolution_multiply_fusion
  183.3 3.2 %fusion.3 = bf16[128,4096]{1,0:T(8,128)(2,1)} fusion(bf16[128,4096]{1,0:T(8,128)(2,1)S(1)} %copy-done.1, f32[128,4096]{1,0:T(8,128)} %get-tuple-element.22, f32[128]{0:T(128)S(1)} %broadcast_multiply_fusion, f32[128]{0:T(128)S(1)} %copy-done.10, f32[4096]{0:T(1024)S(1)} %convert_element_type.53, f32[128]{0:T(128)S(1)} %copy-done.12), kind=kLoop, calls=%fused_computation.8 | loop fusion | flops 3670016 | bytes 4212224 | tf_op jit(solution)/shard_map/convert_element_type | solution.py:78
  (38 shorter events, 0.1 us)
Async XLA Ops:
  7.2 112.1 %copy-start = (bf16[1024,1024]{1,0:T(8,128)(2,1)S(1)}, bf16[1024,1024]{1,0:T(8,128)(2,1)}, u32[]{:S(2)}) copy-start(bf16[1024,1024]{1,0:T(8,128)(2,1)} %param.13) | copy-start | bytes 6291460
  7.2 23.9 %copy-start.1 = (bf16[128,4096]{1,0:T(8,128)(2,1)S(1)}, bf16[128,4096]{1,0:T(8,128)(2,1)}, u32[]{:S(2)}) copy-start(bf16[128,4096]{1,0:T(8,128)(2,1)} %param.10) | copy-start | bytes 3145732
  7.2 75.6 %all-reduce.6.cloned.1.call-start = ((), (), s32[]{:S(2)}) async-start(), calls=%async_computation.2 | async-start | bytes 1867776 | tf_op jit(solution)/shard_map/psum | solution.py:24
  7.2 23.8 %copy-start.15 = (s32[1,128]{1,0:T(1,128)S(1)}, s32[1,128]{1,0:T(1,128)}, u32[]{:S(2)}) copy-start(s32[1,128]{1,0:T(1,128)} %param.11) | copy-start | bytes 1540
  9.5 21.5 %copy-start.11 = (f32[128]{0:T(128)}, f32[128]{0:T(128)S(1)}, u32[]{:S(2)}) copy-start(f32[128]{0:T(128)S(1)} %get-tuple-element.19) | copy-start | bytes 1540
  32.4 154.0 %reduce-scatter.2.cloned.1.call-start = ((), (), s32[]{:S(2)}) async-start(), calls=%async_computation.1 | async-start | bytes 4718592 | tf_op jit(solution)/shard_map/reduce_scatter | solution.py:79
  85.5 1.7 copy-start.5
  85.5 1.7 copy-start.8
  87.2 0.6 copy-start.2
  91.7 0.7 copy-start.7
  91.7 0.7 copy-start.9
  91.8 0.7 copy-start.14
  91.8 1.3 copy-start.6
  91.8 15.3 %copy-start.3 = (bf16[48,256]{1,0:T(8,128)(2,1)S(1)}, bf16[48,256]{1,0:T(8,128)(2,1)}, u32[]{:S(2)}) copy-start(bf16[48,256]{1,0:T(8,128)(2,1)} %copy-done.2) | copy-start | bytes 73732
  91.8 45.8 %copy-start.12 = (f32[128]{0:T(128)S(1)}, f32[128]{0:T(128)}, u32[]{:S(2)}) copy-start(f32[128]{0:T(128)} %copy-done.11) | copy-start | bytes 1540
  91.8 45.8 %copy-start.13 = (f32[48]{0:T(128)S(1)}, f32[48]{0:T(128)}, u32[]{:S(2)}) copy-start(f32[48]{0:T(128)} %psum.45) | copy-start | bytes 580
  91.8 45.8 %copy-start.16 = (s32[1,128]{1,0:T(1,128)S(1)}, s32[1,128]{1,0:T(1,128)}, u32[]{:S(2)}) copy-start(s32[1,128]{1,0:T(1,128)} %param.11) | copy-start | bytes 1540
  137.6 44.9 %copy-start.4 = (f32[48,384]{1,0:T(8,128)S(1)}, f32[48,384]{1,0:T(8,128)}, u32[]{:S(2)}) copy-start(f32[48,384]{1,0:T(8,128)} %get-tuple-element.14) | copy-start | bytes 221188
  137.6 45.7 %copy-start.10 = (f32[128]{0:T(128)S(1)}, f32[128]{0:T(128)}, u32[]{:S(2)}) copy-start(f32[128]{0:T(128)} %get-tuple-element.18) | copy-start | bytes 1540
Sparse Core Ops, SparseCore 0:
  32.6 50.2 all-reduce.5
  91.9 50.7 reduce-scatter.1
where the time goes:
time: 195 us; the launch traced here: 194 us
  blocking collectives  113 us (58%)
  waiting for transfers between devices  37.4 us (19%)
  between operations  16.6 us (9%)
  matrix products  14.5 us (7%)
  other arithmetic  10.8 us (6%)
  local copies, waits for them, and re-layouts  2.47 us (1%)
    psum x1, blocking collectives, local(): gain_grad = lax.psum(gain_part, ('dp', 'fsdp'))  42 us
    psum x1, waiting for transfers between devices, local(): scores = lax.psum(partial_value, 'fsdp') * logit_scale  37.4 us
    all_gather x1, blocking collectives, local(): mean_grad = lax.all_gather(mean_part, 'fsdp', axis=1, tiled=True)  17.5 us
    psum x1, blocking collectives, local(): loss_total = lax.psum(loss_local, 'dp')  13.3 us
    all_gather x1, blocking collectives, local(): grad_full = lax.all_gather(grad_low, 'fsdp', axis=1, tiled=True)  12.2 us
    psum x1, blocking collectives, local(): pooled, counts = lax.psum((pooled_part, counts_part), 'fsdp')  9.73 us
    all_gather x1, blocking collectives, local(): lax.all_gather(query_cache, 'dp', axis=0, tiled=True)  9.23 us
    all_gather x1, blocking collectives, local(): lax.all_gather(region_cache, 'dp', axis=0, tiled=True)  8.47 us
  transfers between devices with their start and end apart: 2, of which 1 were waited for; matrix products, arithmetic and copies ran while one was open for 6% of the time, Pallas kernels for 0%

commit v1 on v0

--- a/solution.py
+++ b/solution.py
@@ -83,7 +83,7 @@
         tiled=True,
     )
     loss_total = lax.psum(loss_local, "dp")
-    gain_grad = lax.psum(gain_part, ("dp", "fsdp"))
+    gain_grad = jnp.sum(lax.all_gather(gain_part, ("dp", "fsdp")), axis=0)
     mean_loss = loss_total / pair_count
     return (mean_loss, query_grad, region_grad, hidden_grad, gain_grad, proj_grad)
 

time: 195 us -> 234 us (1.20); the launches traced: 194 us -> 230 us
  blocking collectives: 113 us -> 145 us
    all_gather x0 -> x1, blocking collectives: none -> 74.1 us  [local(): gain_grad = jnp.sum(lax.all_gather(gain_part, ('dp', 'fsdp')), axis=0)]
    psum x1 -> x0, blocking collectives: 42 us -> none  [local(): gain_grad = lax.psum(gain_part, ('dp', 'fsdp'))]
where the time goes in v1:
time: 234 us; the launch traced here: 230 us
  blocking collectives  145 us (62%)
  waiting for transfers between devices  37.4 us (16%)
  between operations  16.6 us (7%)
  matrix products  14.5 us (6%)
  other arithmetic  12.4 us (5%)
  local copies, waits for them, and re-layouts  4.4 us (2%)
    all_gather x1, blocking collectives, local(): gain_grad = jnp.sum(lax.all_gather(gain_part, ('dp', 'fsdp')), axis=0)  74.1 us
    psum x1, waiting for transfers between devices, local(): scores = lax.psum(partial_value, 'fsdp') * logit_scale  37.4 us
    all_gather x1, blocking collectives, local(): mean_grad = lax.all_gather(mean_part, 'fsdp', axis=1, tiled=True)  17.5 us
    psum x1, blocking collectives, local(): loss_total = lax.psum(loss_local, 'dp')  13.3 us
    all_gather x1, blocking collectives, local(): grad_full = lax.all_gather(grad_low, 'fsdp', axis=1, tiled=True)  12.2 us
    psum x1, blocking collectives, local(): pooled, counts = lax.psum((pooled_part, counts_part), 'fsdp')  9.74 us
    all_gather x1, blocking collectives, local(): lax.all_gather(query_cache, 'dp', axis=0, tiled=True)  9.23 us
    all_gather x1, blocking collectives, local(): lax.all_gather(region_cache, 'dp', axis=0, tiled=True)  8.47 us
  transfers between devices with their start and end apart: 2, of which 1 were waited for; matrix products, arithmetic and copies ran while one was open for 6% of the time, Pallas kernels for 0%

profile of v1, /device:TPU:12, one launch (start us, length us, event | category | flops | bytes accessed | tf_op | source)
XLA Modules:
  0.0 230.0 jit_solution(14542525772632597278)
XLA Ops:
  7.2 1.7 fusion
  8.9 0.5 multiply_multiply_fusion
  9.5 0.7 convert_element_type.53
  10.2 9.2 %all_gather.25 = bf16[384,256]{1,0:T(8,128)(2,1)S(1)} all-gather(bf16[48,256]{1,0:T(8,128)(2,1)} %param.7), channel_id=1, replica_groups=mesh['dp'=8,'fsdp'=4] {'dp'}, dimensions={0}, use_global_device_ids=true | all-gather | bytes 221184 | tf_op jit(solution)/shard_map/all_gather | solution.py:19
  19.4 8.5 %all_gather.24 = bf16[384,256]{1,0:T(8,128)(2,1)S(1)} all-gather(bf16[48,256]{1,0:T(8,128)(2,1)} %param.8), channel_id=1, replica_groups=mesh['dp'=8,'fsdp'=4] {'dp'}, dimensions={0}, use_global_device_ids=true | all-gather | bytes 221184 | tf_op jit(solution)/shard_map/all_gather | solution.py:18
  27.9 1.6 fusion.32
  29.4 1.6 fusion.31
  31.0 1.4 fusion.9
  32.4 0.0 reduce-scatter.2.cloned.1.call-start
  32.4 1.2 dynamic-slice
  34.3 1.3 convert_reduce_fusion
  35.6 9.7 %psum.38 = f32[48]{0:T(128)} all-reduce(f32[48]{0:T(128)} %convert_reduce_fusion), channel_id=1, replica_groups=mesh['dp'=8,'fsdp'=4] {'fsdp'}, use_global_device_ids=true, to_apply=%region_9.10 | all-reduce | flops 48 | bytes 384 | tf_op jit(solution)/shard_map/psum | solution.py:59
  45.4 37.4 %all-reduce.6.cloned.1.call-done = (f32[48,384]{1,0:T(8,128)}, f32[48,384]{1,0:T(8,128)}, f32[48,4096]{1,0:T(8,128)}) async-done(((f32[48,384]{1,0:T(8,128)}, f32[48,384]{1,0:T(8,128)}, f32[48,4096]{1,0:T(8,128)}), (f32[48,384]{1,0:T(8,128)}, f32[48,384]{1,0:T(8,128)}, f32[48,4096]{1,0:T(8,128)})) %all-reduce.6.cloned.1.call-update) | async-done | bytes 933904 | tf_op jit(solution)/shard_map/psum | solution.py:24
  82.8 1.0 multiply_reduce_fusion
  83.7 1.6 select_reduce_fusion
  85.4 0.1 fusion.29
  85.5 1.7 fusion.30
  87.2 0.6 copy-done.2
  87.8 3.9 %fusion.15 = f32[4096,256]{1,0:T(8,128)} fusion(bf16[48,256]{1,0:T(8,128)(2,1)S(1)} %get-tuple-element.20, f32[48,4096]{1,0:T(8,128)} %get-tuple-element.15, f32[48]{0:T(128)} %psum.38), kind=kOutput, calls=%fused_computation.22 | convolution fusion | flops 101056512 | bytes 5005504 | tf_op jit(solution)/shard_map/dot_general | solution.py:80
  91.8 0.5 copy-done.7
  92.3 0.1 convert_dynamic-update-slice_fusion
  92.4 0.6 subtract_reduce_fusion
  93.0 13.3 %all-reduce.2 = (f32[]{:T(128)}, f32[384]{0:T(512)S(1)}, f32[384]{0:T(512)S(1)}) all-reduce(f32[]{:T(128)} %subtract_reduce_fusion, f32[384]{0:T(512)S(1)} %convert_dynamic-update-slice_fusion, f32[384]{0:T(512)S(1)} %copy-done.6), channel_id=1, replica_groups=mesh['dp'=8,'fsdp'=4] {'dp'}, use_global_device_ids=true, to_apply=%region_5.6 | all-reduce | flops 769 | bytes 6152 | tf_op jit(solution)/shard_map/psum | solution.py:85
  106.4 12.2 %all_gather.28 = bf16[48,1024]{1,0:T(8,128)(2,1)S(1)} all-gather(bf16[48,256]{1,0:T(8,128)(2,1)S(1)} %copy-done.3), channel_id=1, replica_groups=mesh['dp'=8,'fsdp'=4] {'fsdp'}, dimensions={1}, use_global_device_ids=true | all-gather | bytes 122880 | tf_op jit(solution)/shard_map/all_gather | solution.py:62
  118.5 0.7 fusion.33
  119.3 17.5 %all_gather.29 = f32[48,4096]{1,0:T(8,128)S(1)} all-gather(f32[48,1024]{1,0:T(8,128)S(1)} %fusion.33), channel_id=1, replica_groups=mesh['dp'=8,'fsdp'=4] {'fsdp'}, dimensions={1}, use_global_device_ids=true | all-gather | bytes 983040 | tf_op jit(solution)/shard_map/all_gather | solution.py:66
  136.8 2.8 %fusion.6 = (f32[4096]{0:T(1024)S(1)}, f32[128]{0:T(128)S(1)}, f32[128,4096]{1,0:T(8,128)}) fusion(bf16[128,4096]{1,0:T(8,128)(2,1)S(1)} %copy-done.1, f32[128]{0:T(128)S(1)} %copy-done.12, f32[4096]{0:T(1024)S(1)} %convert_element_type.53, f32[48,4096]{1,0:T(8,128)S(1)} %all_gather.29, f32[48]{0:T(128)S(1)} %copy-done.13, s32[128]{0:T(128)S(1)} %bitcast.13), kind=kOutput, calls=%fused_computation.11 | convolution fusion | flops 305858432 | bytes 3966656 | tf_op jit(solution)/shard_map/dot_general | solution.py:68
  139.7 74.1 %all-gather = f32[131072]{0:T(1024)} all-gather(f32[4096]{0:T(1024)S(1)} %get-tuple-element.6), channel_id=2, replica_groups=mesh['dp'=8,'fsdp'=4] {'dp','fsdp'}, dimensions={0}, use_global_device_ids=true | all-gather | bytes 540672 | tf_op jit(solution)/shard_map/all_gather | solution.py:86
  213.8 1.9 reshape.49
  216.4 1.7 reduce_sum.79
  218.1 0.8 convolution_multiply_fusion
  218.9 3.2 %fusion.3 = bf16[128,4096]{1,0:T(8,128)(2,1)} fusion(bf16[128,4096]{1,0:T(8,128)(2,1)S(1)} %copy-done.1, f32[128,4096]{1,0:T(8,128)} %get-tuple-element.22, f32[128]{0:T(128)S(1)} %broadcast_multiply_fusion, f32[128]{0:T(128)S(1)} %copy-done.10, f32[4096]{0:T(1024)S(1)} %convert_element_type.53, f32[128]{0:T(128)S(1)} %copy-done.12), kind=kLoop, calls=%fused_computation.8 | loop fusion | flops 3670016 | bytes 4212224 | tf_op jit(solution)/shard_map/convert_element_type | solution.py:78
  (40 shorter events, 0.2 us)
Async XLA Ops:
  7.2 111.4 %copy-start = (bf16[1024,1024]{1,0:T(8,128)(2,1)S(1)}, bf16[1024,1024]{1,0:T(8,128)(2,1)}, u32[]{:S(2)}) copy-start(bf16[1024,1024]{1,0:T(8,128)(2,1)} %param.13) | copy-start | bytes 6291460
  7.2 23.8 %copy-start.1 = (bf16[128,4096]{1,0:T(8,128)(2,1)S(1)}, bf16[128,4096]{1,0:T(8,128)(2,1)}, u32[]{:S(2)}) copy-start(bf16[128,4096]{1,0:T(8,128)(2,1)} %param.10) | copy-start | bytes 3145732
  7.2 75.6 %all-reduce.6.cloned.1.call-start = ((), (), s32[]{:S(2)}) async-start(), calls=%async_computation.2 | async-start | bytes 1867776 | tf_op jit(solution)/shard_map/psum | solution.py:24
  7.2 23.7 %copy-start.15 = (s32[1,128]{1,0:T(1,128)S(1)}, s32[1,128]{1,0:T(1,128)}, u32[]{:S(2)}) copy-start(s32[1,128]{1,0:T(1,128)} %param.11) | copy-start | bytes 1540
  9.5 21.5 %copy-start.11 = (f32[128]{0:T(128)}, f32[128]{0:T(128)S(1)}, u32[]{:S(2)}) copy-start(f32[128]{0:T(128)S(1)} %get-tuple-element.19) | copy-start | bytes 1540
  32.4 189.7 %reduce-scatter.2.cloned.1.call-start = ((), (), s32[]{:S(2)}) async-start(), calls=%async_computation.1 | async-start | bytes 4718592 | tf_op jit(solution)/shard_map/reduce_scatter | solution.py:79
  85.4 1.7 copy-start.5
  85.5 1.7 copy-start.8
  87.2 0.6 copy-start.2
  91.7 0.7 copy-start.7
  91.7 0.7 copy-start.9
  91.7 0.7 copy-start.14
  91.7 1.3 copy-start.6
  91.7 14.7 %copy-start.3 = (bf16[48,256]{1,0:T(8,128)(2,1)S(1)}, bf16[48,256]{1,0:T(8,128)(2,1)}, u32[]{:S(2)}) copy-start(bf16[48,256]{1,0:T(8,128)(2,1)} %copy-done.2) | copy-start | bytes 73732
  91.7 45.1 %copy-start.12 = (f32[128]{0:T(128)S(1)}, f32[128]{0:T(128)}, u32[]{:S(2)}) copy-start(f32[128]{0:T(128)} %copy-done.11) | copy-start | bytes 1540
  91.7 45.1 %copy-start.13 = (f32[48]{0:T(128)S(1)}, f32[48]{0:T(128)}, u32[]{:S(2)}) copy-start(f32[48]{0:T(128)} %psum.38) | copy-start | bytes 580
  91.7 45.1 %copy-start.16 = (s32[1,128]{1,0:T(1,128)S(1)}, s32[1,128]{1,0:T(1,128)}, u32[]{:S(2)}) copy-start(s32[1,128]{1,0:T(1,128)} %param.11) | copy-start | bytes 1540
  139.7 78.4 %copy-start.4 = (f32[48,384]{1,0:T(8,128)S(1)}, f32[48,384]{1,0:T(8,128)}, u32[]{:S(2)}) copy-start(f32[48,384]{1,0:T(8,128)} %get-tuple-element.14) | copy-start | bytes 221188
  139.7 79.2 %copy-start.10 = (f32[128]{0:T(128)S(1)}, f32[128]{0:T(128)}, u32[]{:S(2)}) copy-start(f32[128]{0:T(128)} %get-tuple-element.18) | copy-start | bytes 1540
Sparse Core Ops, SparseCore 0:
  32.5 50.2 all-reduce.5
  91.8 50.7 reduce-scatter.1
